TPU v7x, 128 devices: a whole 4x4x4 slice. The times are simulated.
128 devices in a mesh: row: 8 (over x, core), col: 16 (over z, y).
Axes of the slice: x: 4, y: 4, z: 4, core: 2. Of those that a mesh axis runs over, the one named last changes fastest.
Arguments:
- unit_factor: float32 [4, 1024, 2, 2048], P(None, 'row', None, 'col'), may hold values from -0.125 to 0.125
- pivot_inverse: float32 [4, 1024, 2, 2048], P(None, 'row', None, 'col')
- supernode: int32 [32], replicated, may hold values from 0 to 2, never falling along the last dimension, each value on 1 to 16 neighbouring positions
- row_bits: int32 [32, 2], replicated, may hold values 0 or 1
Outputs:
- inverse_blocks: float32 [4, 1024, 2, 2048], P(None, 'row', None, 'col')
Inputs may be any that keep to these rules, and one draw needn't show every extreme that they name: The supernode index never decreases from one block to the next; each supernode has 1 to 16 blocks, one of them exactly 16.
All inputs are finite; a program needn't handle non-finite values.
Results may differ from a plain program's by a relative error of at most 0.0001.
Values sent between devices are 32-bit elements; how exact they have to be, the bound alone decides.
No kernel may reach another device: no remote copies, remote signals or barrier semaphores. Data moves between devices by JAX's collectives and lax.ppermute only.
A program may use at most 128 MiB of HBM per device.

v0:
```python
import jax
import jax.numpy as jnp
from jax import lax
from jax.sharding import PartitionSpec as P

SUPERNODES = 3


def pick(table, index):
    hits = index[:, None] == jnp.arange(table.shape[0])[None, :]
    return jnp.sum(jnp.where(hits, table[None, :], 0.0), axis=1)


def shards(unit_factor, pivot_inverse, supernode, row_bits):
    n_row = lax.axis_size("row")
    n_col = lax.axis_size("col")
    brows, width, bcols, _ = unit_factor.shape
    whole = brows * n_row * width
    row_ids = jnp.arange(brows) * n_row + lax.axis_index("row")
    col_ids = jnp.arange(bcols) * n_col + lax.axis_index("col")
    highest = lax.Precision.HIGHEST

    def member_of(level):
        return (supernode == level).astype(jnp.float32)

    def local_mask(for_rows, for_cols):
        return (
            pick(for_rows, row_ids)[:, None, None, None]
            * pick(for_cols, col_ids)[None, None, :, None]
        )

    last = SUPERNODES - 1
    inverse = pivot_inverse * local_mask(member_of(last), member_of(last))
    column_panel = lax.all_gather(unit_factor, "row", axis=1, tiled=True).reshape(
        whole, bcols * width
    )
    row_panel = lax.all_gather(unit_factor, "col", axis=3, tiled=True).reshape(brows * width, whole)
    for level in range(last - 1, -1, -1):
        member = member_of(level)
        inside = jnp.logical_and(supernode > level, jnp.all(row_bits[:, level:] == 1, axis=1))
        struct = inside.astype(jnp.float32)
        ancestors = inverse * local_mask(struct, struct)
        ucols = (
            column_panel
            * jnp.repeat(struct, width)[:, None]
            * jnp.repeat(pick(member, col_ids), width)[None, :]
        )
        urows = (
            row_panel
            * jnp.repeat(pick(struct, row_ids), width)[:, None]
            * jnp.repeat(member, width)[None, :]
        )
        stacked = ucols.reshape(bcols, n_col * width, bcols * width)
        spread = urows.reshape(brows * width, brows, n_row * width)
        flat_ancestors = ancestors.reshape(brows * width, bcols * width)
        image = jnp.einsum(
            "kajp,jpl->kal",
            lax.all_gather(ancestors, "col", axis=3, tiled=True),
            stacked,
            precision=highest,
            preferred_element_type=jnp.float32,
        )
        flat_image = image.reshape(brows * width, bcols * width)
        update = lax.psum_scatter(
            jnp.einsum(
                "hkp,hl->pkl",
                spread,
                flat_image - flat_ancestors,
                precision=highest,
                preferred_element_type=jnp.float32,
            ),
            "row",
            scatter_dimension=0,
            tiled=True,
        )
        update = jnp.transpose(update, (1, 0, 2)).reshape(brows, width, bcols, width)
        inverse = (
            inverse
            - image.reshape(brows, width, bcols, width)
            + update
            + pivot_inverse * local_mask(member, member)
        )
    return inverse


def solution(mesh):
    in_specs = (P(None, "row", None, "col"), P(None, "row", None, "col"), P(), P())
    out_specs = P(None, "row", None, "col")
    return jax.shard_map(shards, mesh=mesh, in_specs=in_specs, out_specs=out_specs, check_vma=False)
```

profile of v0, /device:TPU:0, one launch (start us, length us, event | category | flops | bytes accessed | tf_op | source)
XLA Modules:
  0.0 454.2 jit_solution(7438462885738137960)
XLA Ops:
  6.5 0.7 all-gather.7.cloned.1.call-update
  7.3 0.7 all-gather.9.cloned.1.call-update
  8.1 0.7 compare_reduce_fusion
  8.8 0.7 compare_convert_fusion.2
  9.5 0.2 select_reduce_fusion
  9.7 0.3 select_reduce_fusion.5
  10.0 0.1 broadcast_multiply_fusion.4
  10.1 2.0 multiply_multiply_fusion.2
  12.0 0.0 reduce-scatter.3.cloned.1.call-start
  12.1 1.2 copy.34
  13.3 0.1 broadcast_in_dim.178
  13.4 0.1 broadcast_in_dim.183
  13.5 0.1 broadcast_in_dim.193
  13.6 0.2 copy.35
  13.8 0.1 broadcast_bitcast_fusion.1
  13.9 0.1 broadcast_in_dim.184
  14.0 0.1 broadcast_in_dim.194
  14.1 0.1 broadcast_bitcast_fusion.3
  14.1 29.4 %all-gather.7.cloned.1.call-done = f32[4,1024,2,128]{3,2,1,0:T(2,128)} async-done(((f32[4,128,2,128]{3,2,1,0:T(2,128)}), f32[4,1024,2,128]{3,2,1,0:T(2,128)}) %all-gather.7.cloned.1.call-update) | async-done | bytes 4194320 | tf_op jit(solution)/shard_map/all_gather | solution.py:34
  43.6 6.5 %reshape.289 = f32[2,2048,256]{2,1,0:T(8,128)} reshape(f32[4,1024,2,128]{3,2,1,0:T(2,128)} %all-gather.7.cloned.1.call-done) | data formatting | bytes 8388608 | tf_op jit(solution)/shard_map/reshape | solution.py:34
  50.0 113.4 %all-gather.9.cloned.1.call-done = f32[4,128,2,2048]{3,2,1,0:T(2,128)} async-done(((f32[4,128,2,128]{3,2,1,0:T(2,128)}), f32[4,128,2,2048]{3,2,1,0:T(2,128)}) %all-gather.9.cloned.1.call-update) | async-done | bytes 8388624 | tf_op jit(solution)/shard_map/all_gather | solution.py:37
  163.4 10.5 %multiply_multiply_fusion = (f32[4,128,2,2048]{3,2,1,0:T(2,128)}, f32[4,128,2,2048]{3,2,1,0:T(2,128)}) fusion(f32[4,128,2,2048]{3,2,1,0:T(2,128)} %all-gather.9.cloned.1.call-done, f32[4]{0:T(128)S(1)} %get-tuple-element.6, f32[2,2048]{1,0:T(2,128)S(1)} %mul.288, f32[2,2048]{1,0:T(2,128)S(1)} %mul.267, f32[4]{0:T(128)S(1)} %get-tuple-element.8), kind=kLoop, calls=%fused_computation.4 | loop fusion | flops 8388608 | bytes 25198624 | tf_op jit(solution)/shard_map/mul | solution.py:49
  173.9 12.4 %mul.270 = f32[512,4,1024]{2,1,0:T(4,128)} reshape(f32[4,128,2,2048]{3,2,1,0:T(2,128)} %get-tuple-element.16) | data formatting | bytes 16777216 | tf_op jit(solution)/shard_map/mul | solution.py:49
  186.4 57.4 %all-gather.5.cloned.1.call-done = f32[4,128,2,2048]{3,1,2,0:T(8,128)} async-done(((f32[4,128,2,128]{3,1,2,0:T(8,128)}), f32[4,128,2,2048]{3,1,2,0:T(8,128)}) %all-gather.5.cloned.1.call-update) | async-done | bytes 8388624 | tf_op jit(solution)/shard_map/all_gather | solution.py:58
  243.8 11.4 %fusion.29 = (f32[4,128,256]{2,1,0:T(8,128)S(1)}, f32[4,128,256]{2,1,0:T(8,128)S(1)}) fusion(f32[4,128,256]{2,1,0:T(8,128)S(1)} %copy.35, f32[4,128,2,2048]{3,1,2,0:T(8,128)} %all-gather.5.cloned.1.call-done, f32[2,2048,256]{2,1,0:T(8,128)} %reshape.289, f32[256]{0:T(256)S(1)} %broadcast_bitcast_fusion.3, f32[2,2048]{1,0:T(2,128)S(1)} %bitcast.70), kind=kOutput, calls=%fused_computation.58 | convolution fusion | flops 6444679168 | bytes 14173184 | tf_op jit(solution)/shard_map/kajp,jpl->kal/dot_general | solution.py:56
  255.2 12.4 %fusion.12 = f32[1024,4,256]{0,2,1:T(8,128)} fusion(f32[512,256,1]{1,0,2:T(8,128)S(1)} %bitcast.63, f32[512,4,1024]{2,1,0:T(4,128)S(1)} %copy-done.1), kind=kOutput, calls=%fused_computation.14 | convolution fusion | flops 6442450944 | bytes 13107200 | tf_op jit(solution)/shard_map/hkp,hl->pkl/dot_general | solution.py:65
  267.7 0.1 broadcast_multiply_fusion.2
  267.8 0.2 copy.32
  268.0 0.2 copy.33
  268.2 36.7 %reduce-scatter.3.cloned.1.call-done = f32[128,4,256]{0,2,1:T(8,128)} async-done(((f32[1024,4,256]{0,2,1:T(8,128)}), f32[128,4,256]{0,2,1:T(8,128)}) %reduce-scatter.3.cloned.1.call-update) | async-done | bytes 524304 | tf_op jit(solution)/shard_map/reduce_scatter | solution.py:64
  304.9 1.2 copy.38
  306.2 1.0 broadcast_multiply_fusion
  307.3 0.1 broadcast_in_dim.188
  307.3 0.1 broadcast_bitcast_fusion
  307.4 0.1 broadcast_bitcast_fusion.2
  307.5 12.6 %mul.291 = f32[512,4,1024]{2,1,0:T(4,128)} reshape(f32[4,128,2,2048]{3,2,1,0:T(2,128)} %get-tuple-element.15) | data formatting | bytes 16777216 | tf_op jit(solution)/shard_map/mul | solution.py:49
  320.1 0.2 copy.42
  320.3 0.2 copy.43
  320.5 63.2 %all-gather.11.cloned.1.call-done = f32[4,128,2,2048]{3,1,2,0:T(8,128)} async-done(((f32[4,128,2,128]{3,1,2,0:T(8,128)}), f32[4,128,2,2048]{3,1,2,0:T(8,128)}) %all-gather.11.cloned.1.call-update) | async-done | bytes 8388624 | tf_op jit(solution)/shard_map/all_gather | solution.py:58
  383.7 11.4 %fusion.30 = (f32[4,128,256]{2,1,0:T(8,128)S(1)}, f32[4,128,256]{2,1,0:T(8,128)S(1)}) fusion(f32[4,128,256]{2,1,0:T(8,128)S(1)} %copy.43, f32[4,128,2,2048]{3,1,2,0:T(8,128)} %all-gather.11.cloned.1.call-done, f32[2,2048,256]{2,1,0:T(8,128)} %reshape.289, f32[256]{0:T(256)S(1)} %broadcast_bitcast_fusion.2, f32[2,2048]{1,0:T(2,128)S(1)} %bitcast.71), kind=kOutput, calls=%fused_computation.59 | convolution fusion | flops 6444679168 | bytes 14173184 | tf_op jit(solution)/shard_map/kajp,jpl->kal/dot_general | solution.py:56
  395.1 12.2 %fusion.15 = f32[1024,4,256]{0,2,1:T(8,128)} fusion(f32[512,256,1]{1,0,2:T(8,128)S(1)} %bitcast.62, f32[512,4,1024]{2,1,0:T(4,128)S(1)} %copy-done), kind=kOutput, calls=%fused_computation.15 | convolution fusion | flops 6442450944 | bytes 13107200 | tf_op jit(solution)/shard_map/hkp,hl->pkl/dot_general | solution.py:65
  407.4 0.1 broadcast_multiply_fusion.1
  407.5 0.2 copy.40
  407.7 0.2 copy.41
  407.9 36.8 %reduce-scatter.5.cloned.1.call-done = f32[128,4,256]{0,2,1:T(8,128)} async-done(((f32[1024,4,256]{0,2,1:T(8,128)}), f32[128,4,256]{0,2,1:T(8,128)}) %reduce-scatter.5.cloned.1.call-update) | async-done | bytes 524304 | tf_op jit(solution)/shard_map/reduce_scatter | solution.py:64
  444.6 1.2 copy.46
  445.9 0.3 multiply_add_fusion
  446.2 1.2 copy.48
  (23 shorter events, 0.3 us)
Async XLA Ops:
  6.5 37.0 %all-gather.7.cloned.1.call-start = ((), (), s32[]{:S(2)}) async-start(), calls=%async_computation.3 | async-start | bytes 4718592 | tf_op jit(solution)/shard_map/all_gather | solution.py:34
  7.3 156.2 %all-gather.9.cloned.1.call-start = ((), (), s32[]{:S(2)}) async-start(), calls=%async_computation.4 | async-start | bytes 8912896 | tf_op jit(solution)/shard_map/all_gather | solution.py:37
  8.0 235.8 %all-gather.5.cloned.1.call-start = ((), (), s32[]{:S(2)}) async-start(), calls=%async_computation.2 | async-start | bytes 8912896 | tf_op jit(solution)/shard_map/all_gather | solution.py:58
  12.0 292.9 %reduce-scatter.3.cloned.1.call-start = ((), (), s32[]{:S(2)}) async-start(), calls=%async_computation.5 | async-start | bytes 4718592 | tf_op jit(solution)/shard_map/reduce_scatter | solution.py:64
  243.8 11.5 %copy-start.1 = (f32[512,4,1024]{2,1,0:T(4,128)S(1)}, f32[512,4,1024]{2,1,0:T(4,128)}, u32[]{:S(2)}) copy-start(f32[512,4,1024]{2,1,0:T(4,128)} %mul.270) | copy-start | bytes 25165828
  255.2 50.9 %copy-start.3 = (f32[4,128,2,128]{3,2,1,0:T(2,128)S(1)}, f32[4,128,2,128]{3,2,1,0:T(2,128)}, u32[]{:S(2)}) copy-start(f32[4,128,2,128]{3,2,1,0:T(2,128)} %param.5) | copy-start | bytes 1572868
  267.7 116.0 %all-gather.11.cloned.1.call-start = ((), (), s32[]{:S(2)}) async-start(), calls=%async_computation.6 | async-start | bytes 8912896 | tf_op jit(solution)/shard_map/all_gather | solution.py:58
  307.2 137.4 %reduce-scatter.5.cloned.1.call-start = ((), (), s32[]{:S(2)}) async-start(), calls=%async_computation.7 | async-start | bytes 4718592 | tf_op jit(solution)/shard_map/reduce_scatter | solution.py:64
  307.5 12.6 %copy-start.2 = (f32[4,128,2,128]{3,1,2,0:T(8,128)S(1)}, f32[4,128,2,128]{3,1,2,0:T(8,128)}, u32[]{:S(2)}) copy-start(f32[4,128,2,128]{3,1,2,0:T(8,128)} %broadcast_multiply_fusion) | copy-start | bytes 1572868
  383.7 11.4 %copy-start = (f32[512,4,1024]{2,1,0:T(4,128)S(1)}, f32[512,4,1024]{2,1,0:T(4,128)}, u32[]{:S(2)}) copy-start(f32[512,4,1024]{2,1,0:T(4,128)} %mul.291) | copy-start | bytes 25165828
Sparse Core Ops, SparseCore 0:
  9.0 34.4 all-gather.6
  45.7 117.7 all-gather.8
  165.6 78.1 all-gather.4
  267.8 37.0 reduce-scatter.2
  307.3 76.3 all-gather.10
  407.5 37.0 reduce-scatter.4
where the time goes:
time: 455 us; the launch traced here: 454 us
  waiting for transfers between devices  338 us (74%)
  matrix products  47.5 us (10%)
  local copies, waits for them, and re-layouts  38.6 us (8%)
  other arithmetic  15.9 us (3%)
  between operations  13.6 us (3%)
    all_gather x2, waiting for transfers between devices, shards(): lax.all_gather(ancestors, 'col', axis=3, tiled=True)  121 us
    all_gather x1, waiting for transfers between devices, shards(): lax.all_gather(unit_factor, 'col', axis=3, tiled=True)  113 us
    reduce_scatter x2, waiting for transfers between devices, shards(): lax.psum_scatter(jnp.einsum('hkp,hl->pkl', spread, flat_image - flat_ance...  73.5 us
    all_gather x1, waiting for transfers between devices, shards(): lax.all_gather(unit_factor, 'row', axis=1, tiled=True)  29.4 us
    mul x4, local copies, waits for them, and re-layouts, shards(): row_panel * jnp.repeat(pick(struct, row_ids), width)[:, None]  25.1 us
    dot_general x2, matrix products, shards(): jnp.einsum('hkp,hl->pkl', spread, flat_image - flat_ancestors, precision=...  24.6 us
    dot_general x2, matrix products, shards(): jnp.einsum('kajp,jpl->kal', lax.all_gather(ancestors, 'col', axis=3, tile...  22.9 us
    mul x1, other arithmetic, shards(): row_panel * jnp.repeat(pick(struct, row_ids), width)[:, None]  10.5 us
  transfers between devices with their start and end apart: 6, of which 6 were waited for; matrix products, arithmetic and copies ran while one was open for 11% of the time, Pallas kernels for 0%

commit v1 on v0

--- a/solution.py
+++ b/solution.py
@@ -4,6 +4,22 @@
 from jax.sharding import PartitionSpec as P
 
 SUPERNODES = 3
+
+
+def summed_both_ways(value, axis, dim, contribution):
+    peers, here, rows = (lax.axis_size(axis), lax.axis_index(axis), value.shape[dim])
+    forward = [(i, (i + 1) % peers) for i in range(peers)]
+    left = [(i, (i - 1) % peers) for i in range(peers)]
+    middle = peers // 2
+    from_left = from_right = value
+    running = contribution(value, here * rows)
+    for step in range(1, middle + 1):
+        from_left = lax.ppermute(from_left, axis, forward)
+        if step < peers - middle:
+            from_right = lax.ppermute(from_right, axis, left)
+            running = running + contribution(from_right, (here + step) % peers * rows)
+        running = running + contribution(from_left, (here - step) % peers * rows)
+    return running
 
 
 def pick(table, index):
@@ -53,12 +69,17 @@
         stacked = ucols.reshape(bcols, n_col * width, bcols * width)
         spread = urows.reshape(brows * width, brows, n_row * width)
         flat_ancestors = ancestors.reshape(brows * width, bcols * width)
-        image = jnp.einsum(
-            "kajp,jpl->kal",
-            lax.all_gather(ancestors, "col", axis=3, tiled=True),
-            stacked,
-            precision=highest,
-            preferred_element_type=jnp.float32,
+        image = summed_both_ways(
+            ancestors,
+            "col",
+            3,
+            lambda own_block, start: jnp.einsum(
+                "kajp,jpl->kal",
+                own_block,
+                lax.dynamic_slice_in_dim(stacked, start, own_block.shape[3], axis=1),
+                precision=highest,
+                preferred_element_type=jnp.float32,
+            ),
         )
         flat_image = image.reshape(brows * width, bcols * width)
         update = lax.psum_scatter(

time: 455 us -> 475 us (1.044); the launches traced: 454 us -> 468 us
  waiting for transfers between devices: 338 us -> 255 us
  starting transfers between devices: 0.21 us -> 79.6 us
  matrix products: 47.5 us -> 61.3 us
    ppermute x0 -> x30, waiting for transfers between devices: none -> 130 us  [the longest x16 119 us: summed_both_ways(): from_left = lax.ppermute(from_left, axis, forward)]
    all_gather x2 -> x0, waiting for transfers between devices: 121 us -> none  [shards(): lax.all_gather(ancestors, 'col', axis=3, tiled=True)]
    ppermute x0 -> x30, starting transfers between devices: none -> 79.5 us  [the longest x14 75.4 us: summed_both_ways(): from_right = lax.ppermute(from_right, axis, left)]
    all_gather x1, waiting for transfers between devices: 113 us -> 46.9 us  [shards(): lax.all_gather(unit_factor, 'col', axis=3, tiled=True)]
    all_gather x1, waiting for transfers between devices: 29.4 us -> 0.02 us  [shards(): lax.all_gather(unit_factor, 'row', axis=1, tiled=True)]
    dot_general x2 -> x32, matrix products: 22.9 us -> 35 us  [shards(): jnp.einsum('kajp,jpl->kal', own_block, lax.dynamic_slice_in_dim(stacked,...]
    mul x0 -> x1, other arithmetic: none -> 5.68 us  [shards(): column_panel * jnp.repeat(struct, width)[:, None]]
  transfers between devices with their start and end apart: 6 -> 34, of which waited for: 6 -> 21; matrix products, arithmetic and copies ran while one was open for 11% -> 14% of each run, Pallas kernels for 0% -> 0%
where the time goes in v1:
time: 475 us; the launch traced here: 468 us
  waiting for transfers between devices  255 us (54%)
  starting transfers between devices  79.6 us (17%)
  matrix products  61.3 us (13%)
  local copies, waits for them, and re-layouts  37.7 us (8%)
  other arithmetic  20 us (4%)
  between operations  14.1 us (3%)
    ppermute x16, waiting for transfers between devices, summed_both_ways(): from_left = lax.ppermute(from_left, axis, forward)  119 us
    reduce_scatter x2, waiting for transfers between devices, shards(): lax.psum_scatter(jnp.einsum('hkp,hl->pkl', spread, flat_image - flat_ance...  76.9 us
    ppermute x14, starting transfers between devices, summed_both_ways(): from_right = lax.ppermute(from_right, axis, left)  75.4 us
    all_gather x1, waiting for transfers between devices, shards(): lax.all_gather(unit_factor, 'col', axis=3, tiled=True)  46.9 us
    dot_general x32, matrix products, shards(): jnp.einsum('kajp,jpl->kal', own_block, lax.dynamic_slice_in_dim(stacked,...  35 us
    dot_general x2, matrix products, shards(): jnp.einsum('hkp,hl->pkl', spread, flat_image - flat_ancestors, precision=...  26.3 us
    mul x4, local copies, waits for them, and re-layouts, shards(): row_panel * jnp.repeat(pick(struct, row_ids), width)[:, None]  25.2 us
    ppermute x14, waiting for transfers between devices, summed_both_ways(): from_right = lax.ppermute(from_right, axis, left)  11.1 us
  transfers between devices with their start and end apart: 34, of which 21 were waited for; matrix products, arithmetic and copies ran while one was open for 14% of the time, Pallas kernels for 0%

profile of v1, /device:TPU:0, one launch (start us, length us, event | category | flops | bytes accessed | tf_op | source)
XLA Modules:
  0.0 468.1 jit_solution(7832454793619783634)
XLA Ops:
  11.2 1.8 collective-permute-start.1
  13.0 5.0 %collective-permute-start = (f32[4,128,2,128]{3,1,2,0:T(8,128)S(1)}, f32[4,128,2,128]{3,1,2,0:T(8,128)S(1)}, u32[]{:S(2)}, u32[]{:S(2)}) collective-permute-start(f32[4,128,2,128]{3,1,2,0:T(8,128)S(1)} %multiply_multiply_fusion.4), channel_id=1, source_target_pairs={{0,15},{1,0},{2,1},{3,2},{4,3},{5,4},{6,5},{7,6},{8,7},{9,8},{10,9... | collective-permute-start | bytes 1572872 | tf_op jit(solution)/shard_map/ppermute | solution.py:19
  18.0 11.8 %collective-permute-done.1 = f32[4,128,2,128]{3,1,2,0:T(8,128)S(1)} collective-permute-done((f32[4,128,2,128]{3,1,2,0:T(8,128)S(1)}, f32[4,128,2,128]{3,1,2,0:T(8,128)S(1)}, u32[]{:S(2)}, u32[]{:S(2)}) %collective-permute-start.1) | collective-permute-done | bytes 524320 | tf_op jit(solution)/shard_map/ppermute | solution.py:17
  29.8 5.3 %collective-permute-start.2 = (f32[4,128,2,128]{3,1,2,0:T(8,128)S(1)}, f32[4,128,2,128]{3,1,2,0:T(8,128)S(1)}, u32[]{:S(2)}, u32[]{:S(2)}) collective-permute-start(f32[4,128,2,128]{3,1,2,0:T(8,128)S(1)} %collective-permute-done), channel_id=1, source_target_pairs={{0,15},{1,0},{2,1},{3,2},{4,3},{5,4},{6,5},{7,6},{8,7},{9,8},{10,9... | collective-permute-start | bytes 1572872 | tf_op jit(solution)/shard_map/ppermute | solution.py:19
  35.2 11.1 %collective-permute-done.3 = f32[4,128,2,128]{3,1,2,0:T(8,128)S(1)} collective-permute-done((f32[4,128,2,128]{3,1,2,0:T(8,128)S(1)}, f32[4,128,2,128]{3,1,2,0:T(8,128)S(1)}, u32[]{:S(2)}, u32[]{:S(2)}) %collective-permute-start.3) | collective-permute-done | bytes 524320 | tf_op jit(solution)/shard_map/ppermute | solution.py:17
  46.2 5.3 %collective-permute-start.4 = (f32[4,128,2,128]{3,1,2,0:T(8,128)S(1)}, f32[4,128,2,128]{3,1,2,0:T(8,128)S(1)}, u32[]{:S(2)}, u32[]{:S(2)}) collective-permute-start(f32[4,128,2,128]{3,1,2,0:T(8,128)S(1)} %collective-permute-done.2), channel_id=1, source_target_pairs={{0,15},{1,0},{2,1},{3,2},{4,3},{5,4},{6,5},{7,6},{8,7},{9,8},{10,9... | collective-permute-start | bytes 1572872 | tf_op jit(solution)/shard_map/ppermute | solution.py:19
  51.6 10.2 %collective-permute-done.5 = f32[4,128,2,128]{3,1,2,0:T(8,128)S(1)} collective-permute-done((f32[4,128,2,128]{3,1,2,0:T(8,128)S(1)}, f32[4,128,2,128]{3,1,2,0:T(8,128)S(1)}, u32[]{:S(2)}, u32[]{:S(2)}) %collective-permute-start.5) | collective-permute-done | bytes 524320 | tf_op jit(solution)/shard_map/ppermute | solution.py:17
  61.8 5.7 %collective-permute-done.4 = f32[4,128,2,128]{3,1,2,0:T(8,128)S(1)} collective-permute-done((f32[4,128,2,128]{3,1,2,0:T(8,128)S(1)}, f32[4,128,2,128]{3,1,2,0:T(8,128)S(1)}, u32[]{:S(2)}, u32[]{:S(2)}) %collective-permute-start.4) | collective-permute-done | bytes 524320 | tf_op jit(solution)/shard_map/ppermute | solution.py:19
  67.5 5.8 %collective-permute-start.6 = (f32[4,128,2,128]{3,1,2,0:T(8,128)S(1)}, f32[4,128,2,128]{3,1,2,0:T(8,128)}, u32[]{:S(2)}, u32[]{:S(2)}) collective-permute-start(f32[4,128,2,128]{3,1,2,0:T(8,128)S(1)} %collective-permute-done.4), channel_id=1, source_target_pairs={{0,15},{1,0},{2,1},{3,2},{4,3},{5,4},{6,5},{7,6},{8,7},{9,8},{10,9... | collective-permute-start | bytes 1572872 | tf_op jit(solution)/shard_map/ppermute | solution.py:19
  73.3 10.9 %collective-permute-done.7 = f32[4,128,2,128]{3,1,2,0:T(8,128)S(1)} collective-permute-done((f32[4,128,2,128]{3,1,2,0:T(8,128)S(1)}, f32[4,128,2,128]{3,1,2,0:T(8,128)S(1)}, u32[]{:S(2)}, u32[]{:S(2)}) %collective-permute-start.7) | collective-permute-done | bytes 524320 | tf_op jit(solution)/shard_map/ppermute | solution.py:17
  84.2 1.8 collective-permute-done.6
  86.0 5.9 %collective-permute-start.8 = (f32[4,128,2,128]{3,1,2,0:T(8,128)}, f32[4,128,2,128]{3,1,2,0:T(8,128)}, u32[]{:S(2)}, u32[]{:S(2)}) collective-permute-start(f32[4,128,2,128]{3,1,2,0:T(8,128)} %collective-permute-done.6), channel_id=1, source_target_pairs={{0,15},{1,0},{2,1},{3,2},{4,3},{5,4},{6,5},{7,6},{8,7},{9,8},{10,9... | collective-permute-start | bytes 1572872 | tf_op jit(solution)/shard_map/ppermute | solution.py:19
  91.9 10.2 %collective-permute-done.9 = f32[4,128,2,128]{3,1,2,0:T(8,128)} collective-permute-done((f32[4,128,2,128]{3,1,2,0:T(8,128)S(1)}, f32[4,128,2,128]{3,1,2,0:T(8,128)}, u32[]{:S(2)}, u32[]{:S(2)}) %collective-permute-start.9) | collective-permute-done | bytes 524320 | tf_op jit(solution)/shard_map/ppermute | solution.py:17
  102.5 5.3 %collective-permute-start.10 = (f32[4,128,2,128]{3,1,2,0:T(8,128)}, f32[4,128,2,128]{3,1,2,0:T(8,128)}, u32[]{:S(2)}, u32[]{:S(2)}) collective-permute-start(f32[4,128,2,128]{3,1,2,0:T(8,128)} %collective-permute-done.8), channel_id=1, source_target_pairs={{0,15},{1,0},{2,1},{3,2},{4,3},{5,4},{6,5},{7,6},{8,7},{9,8},{10,9... | collective-permute-start | bytes 1572872 | tf_op jit(solution)/shard_map/ppermute | solution.py:19
  107.8 10.6 %collective-permute-done.11 = f32[4,128,2,128]{3,1,2,0:T(8,128)} collective-permute-done((f32[4,128,2,128]{3,1,2,0:T(8,128)}, f32[4,128,2,128]{3,1,2,0:T(8,128)}, u32[]{:S(2)}, u32[]{:S(2)}) %collective-permute-start.11) | collective-permute-done | bytes 524320 | tf_op jit(solution)/shard_map/ppermute | solution.py:17
  119.1 5.2 %collective-permute-start.12 = (f32[4,128,2,128]{3,1,2,0:T(8,128)}, f32[4,128,2,128]{3,1,2,0:T(8,128)}, u32[]{:S(2)}, u32[]{:S(2)}) collective-permute-start(f32[4,128,2,128]{3,1,2,0:T(8,128)} %collective-permute-done.10), channel_id=1, source_target_pairs={{0,15},{1,0},{2,1},{3,2},{4,3},{5,4},{6,5},{7,6},{8,7},{9,8},{10,9... | collective-permute-start | bytes 1572872 | tf_op jit(solution)/shard_map/ppermute | solution.py:19
  124.3 9.4 %collective-permute-done.13 = f32[4,128,2,128]{3,1,2,0:T(8,128)} collective-permute-done((f32[4,128,2,128]{3,1,2,0:T(8,128)}, f32[4,128,2,128]{3,1,2,0:T(8,128)}, u32[]{:S(2)}, u32[]{:S(2)}) %collective-permute-start.13) | collective-permute-done | bytes 524320 | tf_op jit(solution)/shard_map/ppermute | solution.py:17
  133.9 6.4 %reshape.289 = f32[2,2048,256]{2,1,0:T(8,128)} reshape(f32[4,1024,2,128]{3,2,1,0:T(2,128)} %all-gather.3.cloned.1.call-done) | data formatting | bytes 8388608 | tf_op jit(solution)/shard_map/reshape | solution.py:50
  140.4 5.7 %multiply_multiply_fusion.2 = (f32[2,2048,256]{2,1,0:T(8,128)}, f32[2,2048,256]{2,1,0:T(8,128)S(1)}) fusion(f32[2,2048,256]{2,1,0:T(8,128)} %reshape.289, f32[256]{0:T(256)S(1)} %get-tuple-element.32, f32[2,2048]{1,0:T(2,128)S(1)} %get-tuple-element.34, f32[256]{0:T(256)S(1)} %get-tuple-element.33, f32[2,2048]{1,0:T(2,128)S(1)} %get-tuple-element.35), kind=kLoop, calls=%fused_computation.6 | loop fusion | flops 4194304 | bytes 12617728 | tf_op jit(solution)/shard_map/mul | solution.py:60
  155.7 1.7 fusion.17
  162.4 1.6 bitcast_subtract_fusion
  164.0 46.9 %all-gather.5.cloned.1.call-done = f32[4,128,2,2048]{3,2,1,0:T(2,128)} async-done(((f32[4,128,2,128]{3,2,1,0:T(2,128)}), f32[4,128,2,2048]{3,2,1,0:T(2,128)}) %all-gather.5.cloned.1.call-update) | async-done | bytes 8388624 | tf_op jit(solution)/shard_map/all_gather | solution.py:53
  210.9 10.5 %multiply_multiply_fusion = (f32[4,128,2,2048]{3,2,1,0:T(2,128)}, f32[4,128,2,2048]{3,2,1,0:T(2,128)}) fusion(f32[4,128,2,2048]{3,2,1,0:T(2,128)} %all-gather.5.cloned.1.call-done, f32[4]{0:T(128)S(1)} %get-tuple-element.6, f32[2,2048]{1,0:T(2,128)S(1)} %mul.368, f32[2,2048]{1,0:T(2,128)S(1)} %mul.347, f32[4]{0:T(128)S(1)} %get-tuple-element.8), kind=kLoop, calls=%fused_computation.4 | loop fusion | flops 8388608 | bytes 25198624 | tf_op jit(solution)/shard_map/mul | solution.py:65
  221.4 12.7 %mul.350 = f32[512,4,1024]{2,1,0:T(4,128)} reshape(f32[4,128,2,2048]{3,2,1,0:T(2,128)} %get-tuple-element.16) | data formatting | bytes 16777216 | tf_op jit(solution)/shard_map/mul | solution.py:65
  234.1 14.2 %fusion.4 = f32[1024,4,256]{0,2,1:T(8,128)} fusion(f32[512,256,1]{1,0,2:T(8,128)S(1)} %bitcast.346, f32[512,4,1024]{2,1,0:T(4,128)} %mul.350), kind=kOutput, calls=%fused_computation.8 | convolution fusion | flops 6442450944 | bytes 13107200 | tf_op jit(solution)/shard_map/hkp,hl->pkl/dot_general | solution.py:86
  248.4 36.3 %reduce-scatter.3.cloned.1.call-done = f32[128,4,256]{0,2,1:T(8,128)} async-done(((f32[1024,4,256]{0,2,1:T(8,128)}), f32[128,4,256]{0,2,1:T(8,128)}) %reduce-scatter.3.cloned.1.call-update) | async-done | bytes 524304 | tf_op jit(solution)/shard_map/reduce_scatter | solution.py:85
  287.7 3.9 collective-permute-start.15
  291.6 8.8 %collective-permute-done.16 = f32[4,128,2,128]{3,1,2,0:T(8,128)S(1)} collective-permute-done((f32[4,128,2,128]{3,1,2,0:T(8,128)S(1)}, f32[4,128,2,128]{3,1,2,0:T(8,128)S(1)}, u32[]{:S(2)}, u32[]{:S(2)}) %collective-permute-start.16) | collective-permute-done | bytes 524320 | tf_op jit(solution)/shard_map/ppermute | solution.py:17
  301.2 5.3 %collective-permute-start.17 = (f32[4,128,2,128]{3,1,2,0:T(8,128)S(1)}, f32[4,128,2,128]{3,1,2,0:T(8,128)}, u32[]{:S(2)}, u32[]{:S(2)}) collective-permute-start(f32[4,128,2,128]{3,1,2,0:T(8,128)S(1)} %collective-permute-done.15), channel_id=1, source_target_pairs={{0,15},{1,0},{2,1},{3,2},{4,3},{5,4},{6,5},{7,6},{8,7},{9,8},{10,9... | collective-permute-start | bytes 1572872 | tf_op jit(solution)/shard_map/ppermute | solution.py:19
  306.5 7.2 %collective-permute-done.18 = f32[4,128,2,128]{3,1,2,0:T(8,128)} collective-permute-done((f32[4,128,2,128]{3,1,2,0:T(8,128)S(1)}, f32[4,128,2,128]{3,1,2,0:T(8,128)}, u32[]{:S(2)}, u32[]{:S(2)}) %collective-permute-start.18) | collective-permute-done | bytes 524320 | tf_op jit(solution)/shard_map/ppermute | solution.py:17
  313.8 5.9 %collective-permute-start.19 = (f32[4,128,2,128]{3,1,2,0:T(8,128)}, f32[4,128,2,128]{3,1,2,0:T(8,128)}, u32[]{:S(2)}, u32[]{:S(2)}) collective-permute-start(f32[4,128,2,128]{3,1,2,0:T(8,128)} %collective-permute-done.17), channel_id=1, source_target_pairs={{0,15},{1,0},{2,1},{3,2},{4,3},{5,4},{6,5},{7,6},{8,7},{9,8},{10,9... | collective-permute-start | bytes 1572872 | tf_op jit(solution)/shard_map/ppermute | solution.py:19
  319.6 12.5 %mul.371 = f32[512,4,1024]{2,1,0:T(4,128)} reshape(f32[4,128,2,2048]{3,2,1,0:T(2,128)} %get-tuple-element.15) | data formatting | bytes 16777216 | tf_op jit(solution)/shard_map/mul | solution.py:65
  333.0 1.8 convolution_bitcast_fusion.15
  334.9 1.7 convolution_bitcast_fusion.13
  336.6 5.1 %collective-permute-start.21 = (f32[4,128,2,128]{3,1,2,0:T(8,128)}, f32[4,128,2,128]{3,1,2,0:T(8,128)S(1)}, u32[]{:S(2)}, u32[]{:S(2)}) collective-permute-start(f32[4,128,2,128]{3,1,2,0:T(8,128)} %collective-permute-done.19), channel_id=1, source_target_pairs={{0,15},{1,0},{2,1},{3,2},{4,3},{5,4},{6,5},{7,6},{8,7},{9,8},{10,9... | collective-permute-start | bytes 1572872 | tf_op jit(solution)/shard_map/ppermute | solution.py:19
  341.7 1.7 fusion.26
  343.4 2.8 collective-permute-done.22
  349.6 5.6 %collective-permute-start.23 = (f32[4,128,2,128]{3,1,2,0:T(8,128)S(1)}, f32[4,128,2,128]{3,1,2,0:T(8,128)S(1)}, u32[]{:S(2)}, u32[]{:S(2)}) collective-permute-start(f32[4,128,2,128]{3,1,2,0:T(8,128)S(1)} %collective-permute-done.21), channel_id=1, source_target_pairs={{0,15},{1,0},{2,1},{3,2},{4,3},{5,4},{6,5},{7,6},{8,7},{9,8},{10,9... | collective-permute-start | bytes 1572872 | tf_op jit(solution)/shard_map/ppermute | solution.py:19
  356.8 3.6 collective-permute-done.24
  360.4 1.7 fusion.30
  363.8 5.8 %collective-permute-start.25 = (f32[4,128,2,128]{3,1,2,0:T(8,128)S(1)}, f32[4,128,2,128]{3,1,2,0:T(8,128)S(1)}, u32[]{:S(2)}, u32[]{:S(2)}) collective-permute-start(f32[4,128,2,128]{3,1,2,0:T(8,128)S(1)} %collective-permute-done.23), channel_id=1, source_target_pairs={{0,15},{1,0},{2,1},{3,2},{4,3},{5,4},{6,5},{7,6},{8,7},{9,8},{10,9... | collective-permute-start | bytes 1572872 | tf_op jit(solution)/shard_map/ppermute | solution.py:19
  370.2 5.5 %collective-permute-done.26 = f32[4,128,2,128]{3,1,2,0:T(8,128)S(1)} collective-permute-done((f32[4,128,2,128]{3,1,2,0:T(8,128)S(1)}, f32[4,128,2,128]{3,1,2,0:T(8,128)S(1)}, u32[]{:S(2)}, u32[]{:S(2)}) %collective-permute-start.26) | collective-permute-done | bytes 524320 | tf_op jit(solution)/shard_map/ppermute | solution.py:17
  377.0 2.4 collective-permute-done.25
  379.4 5.8 %collective-permute-start.27 = (f32[4,128,2,128]{3,1,2,0:T(8,128)S(1)}, f32[4,128,2,128]{3,1,2,0:T(8,128)S(1)}, u32[]{:S(2)}, u32[]{:S(2)}) collective-permute-start(f32[4,128,2,128]{3,1,2,0:T(8,128)S(1)} %collective-permute-done.25), channel_id=1, source_target_pairs={{0,15},{1,0},{2,1},{3,2},{4,3},{5,4},{6,5},{7,6},{8,7},{9,8},{10,9... | collective-permute-start | bytes 1572872 | tf_op jit(solution)/shard_map/ppermute | solution.py:19
  385.8 6.3 %collective-permute-done.28 = f32[4,128,2,128]{3,1,2,0:T(8,128)S(1)} collective-permute-done((f32[4,128,2,128]{3,1,2,0:T(8,128)S(1)}, f32[4,128,2,128]{3,1,2,0:T(8,128)S(1)}, u32[]{:S(2)}, u32[]{:S(2)}) %collective-permute-start.28) | collective-permute-done | bytes 524320 | tf_op jit(solution)/shard_map/ppermute | solution.py:17
  394.1 10.6 %collective-permute-done.29 = f32[4,128,2,128]{3,1,2,0:T(8,128)S(1)} collective-permute-done((f32[4,128,2,128]{3,1,2,0:T(8,128)S(1)}, f32[4,128,2,128]{3,1,2,0:T(8,128)S(1)}, u32[]{:S(2)}, u32[]{:S(2)}) %collective-permute-start.29) | collective-permute-done | bytes 524320 | tf_op jit(solution)/shard_map/ppermute | solution.py:17
  405.4 12.2 %fusion.7 = f32[1024,4,256]{0,2,1:T(8,128)} fusion(f32[512,256,1]{1,0,2:T(8,128)S(1)} %bitcast.347, f32[512,4,1024]{2,1,0:T(4,128)S(1)} %bitcast.345), kind=kOutput, calls=%fused_computation.9 | convolution fusion | flops 6442450944 | bytes 13107200 | tf_op jit(solution)/shard_map/hkp,hl->pkl/dot_general | solution.py:86
  418.0 40.6 %reduce-scatter.5.cloned.1.call-done = f32[128,4,256]{0,2,1:T(8,128)} async-done(((f32[1024,4,256]{0,2,1:T(8,128)}), f32[128,4,256]{0,2,1:T(8,128)}) %reduce-scatter.5.cloned.1.call-update) | async-done | bytes 524304 | tf_op jit(solution)/shard_map/reduce_scatter | solution.py:85
  (115 shorter events, 39.7 us)
Async XLA Ops:
  6.5 127.4 %all-gather.3.cloned.1.call-start = ((), (), s32[]{:S(2)}) async-start(), calls=%async_computation.2 | async-start | bytes 4718592 | tf_op jit(solution)/shard_map/all_gather | solution.py:50
  7.3 203.6 %all-gather.5.cloned.1.call-start = ((), (), s32[]{:S(2)}) async-start(), calls=%async_computation.3 | async-start | bytes 8912896 | tf_op jit(solution)/shard_map/all_gather | solution.py:53
  8.0 276.7 %reduce-scatter.3.cloned.1.call-start = ((), (), s32[]{:S(2)}) async-start(), calls=%async_computation.4 | async-start | bytes 4718592 | tf_op jit(solution)/shard_map/reduce_scatter | solution.py:85
  11.2 18.6 %collective-permute-start.1 = (f32[4,128,2,128]{3,1,2,0:T(8,128)S(1)}, f32[4,128,2,128]{3,1,2,0:T(8,128)S(1)}, u32[]{:S(2)}, u32[]{:S(2)}) collective-permute-start(f32[4,128,2,128]{3,1,2,0:T(8,128)S(1)} %multiply_multiply_fusion.4), channel_id=1, source_target_pairs={{0,1},{1,2},{2,3},{3,4},{4,5},{5,6},{6,7},{7,8},{8,9},{9,10},{10,1... | collective-permute-start | bytes 1572872 | tf_op jit(solution)/shard_map/ppermute | solution.py:17
  13.0 16.8 %collective-permute-start = (f32[4,128,2,128]{3,1,2,0:T(8,128)S(1)}, f32[4,128,2,128]{3,1,2,0:T(8,128)S(1)}, u32[]{:S(2)}, u32[]{:S(2)}) collective-permute-start(f32[4,128,2,128]{3,1,2,0:T(8,128)S(1)} %multiply_multiply_fusion.4), channel_id=1, source_target_pairs={{0,15},{1,0},{2,1},{3,2},{4,3},{5,4},{6,5},{7,6},{8,7},{9,8},{10,9... | collective-permute-start | bytes 1572872 | tf_op jit(solution)/shard_map/ppermute | solution.py:19
  29.8 16.4 %collective-permute-start.3 = (f32[4,128,2,128]{3,1,2,0:T(8,128)S(1)}, f32[4,128,2,128]{3,1,2,0:T(8,128)S(1)}, u32[]{:S(2)}, u32[]{:S(2)}) collective-permute-start(f32[4,128,2,128]{3,1,2,0:T(8,128)S(1)} %collective-permute-done.1), channel_id=1, source_target_pairs={{0,1},{1,2},{2,3},{3,4},{4,5},{5,6},{6,7},{7,8},{8,9},{9,10},{10,1... | collective-permute-start | bytes 1572872 | tf_op jit(solution)/shard_map/ppermute | solution.py:17
  29.8 16.4 %collective-permute-start.2 = (f32[4,128,2,128]{3,1,2,0:T(8,128)S(1)}, f32[4,128,2,128]{3,1,2,0:T(8,128)S(1)}, u32[]{:S(2)}, u32[]{:S(2)}) collective-permute-start(f32[4,128,2,128]{3,1,2,0:T(8,128)S(1)} %collective-permute-done), channel_id=1, source_target_pairs={{0,15},{1,0},{2,1},{3,2},{4,3},{5,4},{6,5},{7,6},{8,7},{9,8},{10,9... | collective-permute-start | bytes 1572872 | tf_op jit(solution)/shard_map/ppermute | solution.py:19
  46.2 15.6 %collective-permute-start.5 = (f32[4,128,2,128]{3,1,2,0:T(8,128)S(1)}, f32[4,128,2,128]{3,1,2,0:T(8,128)S(1)}, u32[]{:S(2)}, u32[]{:S(2)}) collective-permute-start(f32[4,128,2,128]{3,1,2,0:T(8,128)S(1)} %collective-permute-done.3), channel_id=1, source_target_pairs={{0,1},{1,2},{2,3},{3,4},{4,5},{5,6},{6,7},{7,8},{8,9},{9,10},{10,1... | collective-permute-start | bytes 1572872 | tf_op jit(solution)/shard_map/ppermute | solution.py:17
  46.2 21.3 %collective-permute-start.4 = (f32[4,128,2,128]{3,1,2,0:T(8,128)S(1)}, f32[4,128,2,128]{3,1,2,0:T(8,128)S(1)}, u32[]{:S(2)}, u32[]{:S(2)}) collective-permute-start(f32[4,128,2,128]{3,1,2,0:T(8,128)S(1)} %collective-permute-done.2), channel_id=1, source_target_pairs={{0,15},{1,0},{2,1},{3,2},{4,3},{5,4},{6,5},{7,6},{8,7},{9,8},{10,9... | collective-permute-start | bytes 1572872 | tf_op jit(solution)/shard_map/ppermute | solution.py:19
  61.8 24.2 %copy-start.2 = (f32[4,128,2,128]{3,1,2,0:T(8,128)}, f32[4,128,2,128]{3,1,2,0:T(8,128)S(1)}, u32[]{:S(2)}) copy-start(f32[4,128,2,128]{3,1,2,0:T(8,128)S(1)} %collective-permute-done.5) | copy-start | bytes 1572868
  61.8 22.4 %collective-permute-start.7 = (f32[4,128,2,128]{3,1,2,0:T(8,128)S(1)}, f32[4,128,2,128]{3,1,2,0:T(8,128)S(1)}, u32[]{:S(2)}, u32[]{:S(2)}) collective-permute-start(f32[4,128,2,128]{3,1,2,0:T(8,128)S(1)} %collective-permute-done.5), channel_id=1, source_target_pairs={{0,1},{1,2},{2,3},{3,4},{4,5},{5,6},{6,7},{7,8},{8,9},{9,10},{10,1... | collective-permute-start | bytes 1572872 | tf_op jit(solution)/shard_map/ppermute | solution.py:17
  67.5 18.5 %collective-permute-start.6 = (f32[4,128,2,128]{3,1,2,0:T(8,128)S(1)}, f32[4,128,2,128]{3,1,2,0:T(8,128)}, u32[]{:S(2)}, u32[]{:S(2)}) collective-permute-start(f32[4,128,2,128]{3,1,2,0:T(8,128)S(1)} %collective-permute-done.4), channel_id=1, source_target_pairs={{0,15},{1,0},{2,1},{3,2},{4,3},{5,4},{6,5},{7,6},{8,7},{9,8},{10,9... | collective-permute-start | bytes 1572872 | tf_op jit(solution)/shard_map/ppermute | solution.py:19
  84.2 7.8 %copy-start.4 = (f32[4,128,2,128]{3,1,2,0:T(8,128)}, f32[4,128,2,128]{3,1,2,0:T(8,128)S(1)}, u32[]{:S(2)}) copy-start(f32[4,128,2,128]{3,1,2,0:T(8,128)S(1)} %collective-permute-done.7) | copy-start | bytes 1572868
  84.2 18.0 %collective-permute-start.9 = (f32[4,128,2,128]{3,1,2,0:T(8,128)S(1)}, f32[4,128,2,128]{3,1,2,0:T(8,128)}, u32[]{:S(2)}, u32[]{:S(2)}) collective-permute-start(f32[4,128,2,128]{3,1,2,0:T(8,128)S(1)} %collective-permute-done.7), channel_id=1, source_target_pairs={{0,1},{1,2},{2,3},{3,4},{4,5},{5,6},{6,7},{7,8},{8,9},{9,10},{10,1... | collective-permute-start | bytes 1572872 | tf_op jit(solution)/shard_map/ppermute | solution.py:17
  86.0 16.4 %collective-permute-start.8 = (f32[4,128,2,128]{3,1,2,0:T(8,128)}, f32[4,128,2,128]{3,1,2,0:T(8,128)}, u32[]{:S(2)}, u32[]{:S(2)}) collective-permute-start(f32[4,128,2,128]{3,1,2,0:T(8,128)} %collective-permute-done.6), channel_id=1, source_target_pairs={{0,15},{1,0},{2,1},{3,2},{4,3},{5,4},{6,5},{7,6},{8,7},{9,8},{10,9... | collective-permute-start | bytes 1572872 | tf_op jit(solution)/shard_map/ppermute | solution.py:19
  102.2 16.2 %collective-permute-start.11 = (f32[4,128,2,128]{3,1,2,0:T(8,128)}, f32[4,128,2,128]{3,1,2,0:T(8,128)}, u32[]{:S(2)}, u32[]{:S(2)}) collective-permute-start(f32[4,128,2,128]{3,1,2,0:T(8,128)} %collective-permute-done.9), channel_id=1, source_target_pairs={{0,1},{1,2},{2,3},{3,4},{4,5},{5,6},{6,7},{7,8},{8,9},{9,10},{10,1... | collective-permute-start | bytes 1572872 | tf_op jit(solution)/shard_map/ppermute | solution.py:17
  102.5 16.6 %collective-permute-start.10 = (f32[4,128,2,128]{3,1,2,0:T(8,128)}, f32[4,128,2,128]{3,1,2,0:T(8,128)}, u32[]{:S(2)}, u32[]{:S(2)}) collective-permute-start(f32[4,128,2,128]{3,1,2,0:T(8,128)} %collective-permute-done.8), channel_id=1, source_target_pairs={{0,15},{1,0},{2,1},{3,2},{4,3},{5,4},{6,5},{7,6},{8,7},{9,8},{10,9... | collective-permute-start | bytes 1572872 | tf_op jit(solution)/shard_map/ppermute | solution.py:19
  118.4 15.4 %collective-permute-start.13 = (f32[4,128,2,128]{3,1,2,0:T(8,128)}, f32[4,128,2,128]{3,1,2,0:T(8,128)}, u32[]{:S(2)}, u32[]{:S(2)}) collective-permute-start(f32[4,128,2,128]{3,1,2,0:T(8,128)} %collective-permute-done.11), channel_id=1, source_target_pairs={{0,1},{1,2},{2,3},{3,4},{4,5},{5,6},{6,7},{7,8},{8,9},{9,10},{10,1... | collective-permute-start | bytes 1572872 | tf_op jit(solution)/shard_map/ppermute | solution.py:17
  119.1 41.6 %collective-permute-start.12 = (f32[4,128,2,128]{3,1,2,0:T(8,128)}, f32[4,128,2,128]{3,1,2,0:T(8,128)}, u32[]{:S(2)}, u32[]{:S(2)}) collective-permute-start(f32[4,128,2,128]{3,1,2,0:T(8,128)} %collective-permute-done.10), channel_id=1, source_target_pairs={{0,15},{1,0},{2,1},{3,2},{4,3},{5,4},{6,5},{7,6},{8,7},{9,8},{10,9... | collective-permute-start | bytes 1572872 | tf_op jit(solution)/shard_map/ppermute | solution.py:19
  133.7 28.6 %collective-permute-start.14 = (f32[4,128,2,128]{3,1,2,0:T(8,128)}, f32[4,128,2,128]{3,1,2,0:T(8,128)}, u32[]{:S(2)}, u32[]{:S(2)}) collective-permute-start(f32[4,128,2,128]{3,1,2,0:T(8,128)} %collective-permute-done.13), channel_id=1, source_target_pairs={{0,1},{1,2},{2,3},{3,4},{4,5},{5,6},{6,7},{7,8},{8,9},{9,10},{10,1... | collective-permute-start | bytes 1572872 | tf_op jit(solution)/shard_map/ppermute | solution.py:17
  146.0 1.8 copy-start.3
  146.0 2.4 copy-start.5
  155.7 6.6 %copy-start.1 = (f32[4,128,2,128]{3,2,1,0:T(2,128)S(1)}, f32[4,128,2,128]{3,2,1,0:T(2,128)}, u32[]{:S(2)}) copy-start(f32[4,128,2,128]{3,2,1,0:T(2,128)} %param.5) | copy-start | bytes 1572868
  248.3 210.4 %reduce-scatter.5.cloned.1.call-start = ((), (), s32[]{:S(2)}) async-start(), calls=%async_computation.5 | async-start | bytes 4718592 | tf_op jit(solution)/shard_map/reduce_scatter | solution.py:85
  286.2 14.2 %collective-permute-start.16 = (f32[4,128,2,128]{3,1,2,0:T(8,128)S(1)}, f32[4,128,2,128]{3,1,2,0:T(8,128)S(1)}, u32[]{:S(2)}, u32[]{:S(2)}) collective-permute-start(f32[4,128,2,128]{3,1,2,0:T(8,128)S(1)} %broadcast_multiply_fusion), channel_id=1, source_target_pairs={{0,1},{1,2},{2,3},{3,4},{4,5},{5,6},{6,7},{7,8},{8,9},{9,10},{10,1... | collective-permute-start | bytes 1572872 | tf_op jit(solution)/shard_map/ppermute | solution.py:17
  287.7 12.7 %collective-permute-start.15 = (f32[4,128,2,128]{3,1,2,0:T(8,128)S(1)}, f32[4,128,2,128]{3,1,2,0:T(8,128)S(1)}, u32[]{:S(2)}, u32[]{:S(2)}) collective-permute-start(f32[4,128,2,128]{3,1,2,0:T(8,128)S(1)} %broadcast_multiply_fusion), channel_id=1, source_target_pairs={{0,15},{1,0},{2,1},{3,2},{4,3},{5,4},{6,5},{7,6},{8,7},{9,8},{10,9... | collective-permute-start | bytes 1572872 | tf_op jit(solution)/shard_map/ppermute | solution.py:19
  300.4 13.4 %copy-start.7 = (f32[4,128,2,128]{3,1,2,0:T(8,128)}, f32[4,128,2,128]{3,1,2,0:T(8,128)S(1)}, u32[]{:S(2)}) copy-start(f32[4,128,2,128]{3,1,2,0:T(8,128)S(1)} %collective-permute-done.16) | copy-start | bytes 1572868
  300.4 13.4 %collective-permute-start.18 = (f32[4,128,2,128]{3,1,2,0:T(8,128)S(1)}, f32[4,128,2,128]{3,1,2,0:T(8,128)}, u32[]{:S(2)}, u32[]{:S(2)}) collective-permute-start(f32[4,128,2,128]{3,1,2,0:T(8,128)S(1)} %collective-permute-done.16), channel_id=1, source_target_pairs={{0,1},{1,2},{2,3},{3,4},{4,5},{5,6},{6,7},{7,8},{8,9},{9,10},{10,1... | collective-permute-start | bytes 1572872 | tf_op jit(solution)/shard_map/ppermute | solution.py:17
  300.4 0.8 copy-start.6
  301.2 12.5 %collective-permute-start.17 = (f32[4,128,2,128]{3,1,2,0:T(8,128)S(1)}, f32[4,128,2,128]{3,1,2,0:T(8,128)}, u32[]{:S(2)}, u32[]{:S(2)}) collective-permute-start(f32[4,128,2,128]{3,1,2,0:T(8,128)S(1)} %collective-permute-done.15), channel_id=1, source_target_pairs={{0,15},{1,0},{2,1},{3,2},{4,3},{5,4},{6,5},{7,6},{8,7},{9,8},{10,9... | collective-permute-start | bytes 1572872 | tf_op jit(solution)/shard_map/ppermute | solution.py:19
  313.8 18.8 %collective-permute-start.20 = (f32[4,128,2,128]{3,1,2,0:T(8,128)}, f32[4,128,2,128]{3,1,2,0:T(8,128)}, u32[]{:S(2)}, u32[]{:S(2)}) collective-permute-start(f32[4,128,2,128]{3,1,2,0:T(8,128)} %collective-permute-done.18), channel_id=1, source_target_pairs={{0,1},{1,2},{2,3},{3,4},{4,5},{5,6},{6,7},{7,8},{8,9},{9,10},{10,1... | collective-permute-start | bytes 1572872 | tf_op jit(solution)/shard_map/ppermute | solution.py:17
  313.8 22.8 %collective-permute-start.19 = (f32[4,128,2,128]{3,1,2,0:T(8,128)}, f32[4,128,2,128]{3,1,2,0:T(8,128)}, u32[]{:S(2)}, u32[]{:S(2)}) collective-permute-start(f32[4,128,2,128]{3,1,2,0:T(8,128)} %collective-permute-done.17), channel_id=1, source_target_pairs={{0,15},{1,0},{2,1},{3,2},{4,3},{5,4},{6,5},{7,6},{8,7},{9,8},{10,9... | collective-permute-start | bytes 1572872 | tf_op jit(solution)/shard_map/ppermute | solution.py:19
  332.5 13.7 %copy-start = (f32[2,2048,256]{2,1,0:T(8,128)S(1)}, f32[2,2048,256]{2,1,0:T(8,128)}, u32[]{:S(2)}) copy-start(f32[2,2048,256]{2,1,0:T(8,128)} %get-tuple-element.17) | copy-start | bytes 12582916
  332.6 13.7 %collective-permute-start.22 = (f32[4,128,2,128]{3,1,2,0:T(8,128)}, f32[4,128,2,128]{3,1,2,0:T(8,128)S(1)}, u32[]{:S(2)}, u32[]{:S(2)}) collective-permute-start(f32[4,128,2,128]{3,1,2,0:T(8,128)} %collective-permute-done.20), channel_id=1, source_target_pairs={{0,1},{1,2},{2,3},{3,4},{4,5},{5,6},{6,7},{7,8},{8,9},{9,10},{10,1... | collective-permute-start | bytes 1572872 | tf_op jit(solution)/shard_map/ppermute | solution.py:17
  336.6 13.0 %collective-permute-start.21 = (f32[4,128,2,128]{3,1,2,0:T(8,128)}, f32[4,128,2,128]{3,1,2,0:T(8,128)S(1)}, u32[]{:S(2)}, u32[]{:S(2)}) collective-permute-start(f32[4,128,2,128]{3,1,2,0:T(8,128)} %collective-permute-done.19), channel_id=1, source_target_pairs={{0,15},{1,0},{2,1},{3,2},{4,3},{5,4},{6,5},{7,6},{8,7},{9,8},{10,9... | collective-permute-start | bytes 1572872 | tf_op jit(solution)/shard_map/ppermute | solution.py:19
  346.3 14.2 %collective-permute-start.24 = (f32[4,128,2,128]{3,1,2,0:T(8,128)S(1)}, f32[4,128,2,128]{3,1,2,0:T(8,128)S(1)}, u32[]{:S(2)}, u32[]{:S(2)}) collective-permute-start(f32[4,128,2,128]{3,1,2,0:T(8,128)S(1)} %collective-permute-done.22), channel_id=1, source_target_pairs={{0,1},{1,2},{2,3},{3,4},{4,5},{5,6},{6,7},{7,8},{8,9},{9,10},{10,1... | collective-permute-start | bytes 1572872 | tf_op jit(solution)/shard_map/ppermute | solution.py:17
  349.6 14.2 %collective-permute-start.23 = (f32[4,128,2,128]{3,1,2,0:T(8,128)S(1)}, f32[4,128,2,128]{3,1,2,0:T(8,128)S(1)}, u32[]{:S(2)}, u32[]{:S(2)}) collective-permute-start(f32[4,128,2,128]{3,1,2,0:T(8,128)S(1)} %collective-permute-done.21), channel_id=1, source_target_pairs={{0,15},{1,0},{2,1},{3,2},{4,3},{5,4},{6,5},{7,6},{8,7},{9,8},{10,9... | collective-permute-start | bytes 1572872 | tf_op jit(solution)/shard_map/ppermute | solution.py:19
  360.4 15.3 %collective-permute-start.26 = (f32[4,128,2,128]{3,1,2,0:T(8,128)S(1)}, f32[4,128,2,128]{3,1,2,0:T(8,128)S(1)}, u32[]{:S(2)}, u32[]{:S(2)}) collective-permute-start(f32[4,128,2,128]{3,1,2,0:T(8,128)S(1)} %collective-permute-done.24), channel_id=1, source_target_pairs={{0,1},{1,2},{2,3},{3,4},{4,5},{5,6},{6,7},{7,8},{8,9},{9,10},{10,1... | collective-permute-start | bytes 1572872 | tf_op jit(solution)/shard_map/ppermute | solution.py:17
  363.8 15.6 %collective-permute-start.25 = (f32[4,128,2,128]{3,1,2,0:T(8,128)S(1)}, f32[4,128,2,128]{3,1,2,0:T(8,128)S(1)}, u32[]{:S(2)}, u32[]{:S(2)}) collective-permute-start(f32[4,128,2,128]{3,1,2,0:T(8,128)S(1)} %collective-permute-done.23), channel_id=1, source_target_pairs={{0,15},{1,0},{2,1},{3,2},{4,3},{5,4},{6,5},{7,6},{8,7},{9,8},{10,9... | collective-permute-start | bytes 1572872 | tf_op jit(solution)/shard_map/ppermute | solution.py:19
  369.6 35.7 %slice-start = ((s8[8388608]{0:T(1024)(128)(4,1)}), s8[4194304]{0:T(1024)(128)(4,1)S(1)}, s32[]{:S(2)}) async-start(s8[8388608]{0:T(1024)(128)(4,1)} %bitcast.344), calls=%async_computation.6 | async-start | bytes 8388608
  375.8 16.3 %collective-permute-start.28 = (f32[4,128,2,128]{3,1,2,0:T(8,128)S(1)}, f32[4,128,2,128]{3,1,2,0:T(8,128)S(1)}, u32[]{:S(2)}, u32[]{:S(2)}) collective-permute-start(f32[4,128,2,128]{3,1,2,0:T(8,128)S(1)} %collective-permute-done.26), channel_id=1, source_target_pairs={{0,1},{1,2},{2,3},{3,4},{4,5},{5,6},{6,7},{7,8},{8,9},{9,10},{10,1... | collective-permute-start | bytes 1572872 | tf_op jit(solution)/shard_map/ppermute | solution.py:17
  379.4 14.1 %collective-permute-start.27 = (f32[4,128,2,128]{3,1,2,0:T(8,128)S(1)}, f32[4,128,2,128]{3,1,2,0:T(8,128)S(1)}, u32[]{:S(2)}, u32[]{:S(2)}) collective-permute-start(f32[4,128,2,128]{3,1,2,0:T(8,128)S(1)} %collective-permute-done.25), channel_id=1, source_target_pairs={{0,15},{1,0},{2,1},{3,2},{4,3},{5,4},{6,5},{7,6},{8,7},{9,8},{10,9... | collective-permute-start | bytes 1572872 | tf_op jit(solution)/shard_map/ppermute | solution.py:19
  385.8 19.6 %slice-start.1 = ((s8[8388608]{0:T(1024)(128)(4,1)}), s8[4194304]{0:T(1024)(128)(4,1)S(1)}, s32[]{:S(2)}) async-start(s8[8388608]{0:T(1024)(128)(4,1)} %bitcast.344), calls=%async_computation.7 | async-start | bytes 8388608
  392.1 12.7 %collective-permute-start.29 = (f32[4,128,2,128]{3,1,2,0:T(8,128)S(1)}, f32[4,128,2,128]{3,1,2,0:T(8,128)S(1)}, u32[]{:S(2)}, u32[]{:S(2)}) collective-permute-start(f32[4,128,2,128]{3,1,2,0:T(8,128)S(1)} %collective-permute-done.28), channel_id=1, source_target_pairs={{0,1},{1,2},{2,3},{3,4},{4,5},{5,6},{6,7},{7,8},{8,9},{9,10},{10,1... | collective-permute-start | bytes 1572872 | tf_op jit(solution)/shard_map/ppermute | solution.py:17
Sparse Core Ops, SparseCore 0:
  9.0 34.4 all-gather.2
  45.7 165.1 all-gather.4
  248.4 36.2 reduce-scatter.2
  417.7 40.9 reduce-scatter.4
